TPU v7x, 256 devices: a whole 4x4x8 slice. The times are simulated.
256 devices in a mesh: dp: 4 (over z_hi), expert: 16 (over y, z_lo, core), mp: 4 (over x).
Axes of the slice: x: 4, y: 4, z: 8 (z_hi: 4, z_lo: 2; z = z_hi * 2 + z_lo), core: 2. Of those that a mesh axis runs over, the one named last changes fastest.
Arguments:
- hidden: bfloat16 [16384, 2048], P(('dp', 'expert', 'mp')), may hold values from -6 to 6
- norm_gain: float32 [2048], replicated, may hold values from 0.1 to 1.9
- expert_in: float32 [64, 2048, 2816], P('dp', ('expert', 'mp')), may hold values from -0.125 to 0.125
- expert_out: float32 [64, 2048, 1408], P('dp', ('expert', 'mp')), may hold values from -0.15625 to 0.15625
- expert_ids: int32 [16384, 6], P(('dp', 'expert', 'mp')), may hold values from 0 to 63, all different within a row; in each aligned block of 64 rows (0 to 63, 64 to 127, ...) at most 12 rows name the same one
- gate_levels: int32 [16384, 6], P(('dp', 'expert', 'mp')), may hold values from 1 to 255
- shared_gate: bfloat16 [2048, 2816], P(('dp', 'expert'), 'mp'), may hold values from -0.125 to 0.125
- shared_up: bfloat16 [2048, 2816], P(('dp', 'expert'), 'mp'), may hold values from -0.125 to 0.125
- shared_down: bfloat16 [2048, 2816], P(('dp', 'expert'), 'mp'), may hold values from -0.109375 to 0.109375
- next_gain: float32 [2048], replicated, may hold values from 0.1 to 1.9
- kv_weight: bfloat16 [2048, 576], P(None, 'mp'), may hold values from -0.125 to 0.125
Outputs:
- layer_out: bfloat16 [16384, 2048], P(('dp', 'expert', 'mp'))
- kv_latent: bfloat16 [16384, 576], P(('dp', 'expert'), 'mp')
Inputs may be any that keep to these rules, and one draw needn't show every extreme that they name: `expert_ids`: each row names 6 different experts. Among the 64 rows of one device no expert is named by more than 12 rows, and in every draw some expert is named by exactly 12 rows of some device.
All inputs are finite; a program needn't handle non-finite values.
Results may differ from a plain program's by a relative error of at most 0.012.
Values may be sent and summed in bfloat16 or wider, within the bound.
No kernel may reach another device: no remote copies, remote signals or barrier semaphores. Data moves between devices by JAX's collectives and lax.ppermute only.
A program may use at most 128 MiB of HBM per device.

v0:
```python
import jax
import jax.numpy as jnp
from jax import lax
from jax.sharding import PartitionSpec as P


def rms_scale(values, gain):
    wide = values.astype(jnp.float32)
    mean_sq = jnp.mean(wide * wide, axis=-1, keepdims=True)
    return (wide * lax.rsqrt(mean_sq + 1e-06) * gain).astype(jnp.bfloat16)


def expert_part(rows, gate_up_w, down_w):
    quarter = down_w.shape[1]
    gate_up = jnp.dot(rows, gate_up_w, preferred_element_type=jnp.float32)
    act = (jax.nn.silu(gate_up[:, :quarter]) * gate_up[:, quarter:]).astype(jnp.bfloat16)
    return lax.dot_general(
        act, down_w, (((1,), (1,)), ((), ())), preferred_element_type=jnp.float32
    )


def on_device(
    hidden,
    norm_gain,
    expert_in,
    expert_out,
    expert_ids,
    gate_levels,
    shared_gate,
    shared_up,
    shared_down,
    next_gain,
    kv_weight,
):
    tok_rows, width = hidden.shape
    top = expert_ids.shape[1]
    n_mp = lax.axis_size("mp")
    n_groups = lax.axis_size(("dp", "expert"))
    capacity = min(tok_rows, (2 * tok_rows * top + n_groups - 1) // n_groups)
    local_e, local_rows, double = expert_in.shape
    full_ff = double // 2
    quarter = full_ff // n_mp
    in_cast = (
        expert_in.astype(jnp.bfloat16)
        .reshape(local_e, local_rows, 2, n_mp, quarter)
        .transpose(0, 3, 1, 2, 4)
    )
    out_cast = (
        expert_out.astype(jnp.bfloat16)
        .reshape(local_e, local_rows, n_mp, quarter)
        .transpose(0, 2, 1, 3)
    )
    in_send = in_cast.reshape(local_e * n_mp, local_rows, 2, quarter)
    out_send = out_cast.reshape(local_e * n_mp, local_rows, quarter)
    in_recv, out_recv = (
        lax.all_to_all(in_send, ("expert", "mp"), split_axis=0, concat_axis=1, tiled=True),
        lax.all_to_all(out_send, ("expert", "mp"), split_axis=0, concat_axis=1, tiled=True),
    )
    gate_up_w = in_recv.reshape(width, 2 * quarter)
    down_w = out_recv.reshape(width, quarter)
    normed = rms_scale(hidden, norm_gain)
    levels = gate_levels.astype(jnp.float32)
    gate_weights = levels / jnp.sum(levels, axis=1, keepdims=True)
    flat_ids = expert_ids.reshape(-1)
    pairs = flat_ids.shape[0]
    onehot = (flat_ids[:, None] == jnp.arange(n_groups, dtype=jnp.int32)[None, :]).astype(jnp.int32)
    before = jnp.cumsum(onehot, axis=0) - onehot
    slot_of_pair = jnp.sum(before * onehot, axis=1)
    target = flat_ids * capacity + slot_of_pair
    token_of_pair = jnp.arange(pairs, dtype=jnp.int32) // top
    slot_ids = jnp.arange(n_groups * capacity, dtype=jnp.int32)
    token_slot = target.reshape(tok_rows, top)[:, :, None] == slot_ids[None, None, :]
    slot_token = jnp.any(token_slot, axis=1).astype(jnp.bfloat16)
    send = lax.dot_general(
        slot_token, normed, (((0,), (0,)), ((), ())), preferred_element_type=jnp.float32
    ).astype(jnp.bfloat16)
    bounds = (0, 2 * capacity // 3, capacity) if capacity >= 3 else (0, capacity)
    spans = list(zip(bounds[:-1], bounds[1:]))
    send = send.reshape(n_groups, capacity, width)
    received = [
        lax.all_to_all(send[:, lo:hi], ("dp", "expert"), split_axis=0, concat_axis=0, tiled=True)
        for lo, hi in spans
    ]
    shared_cols = shared_gate.shape[1]
    shared_cat = jnp.concatenate([shared_gate, shared_up, shared_down], axis=1)
    shared_cat = lax.all_gather(shared_cat, "dp", axis=0, tiled=False)
    shared_cat = lax.all_gather(shared_cat, "expert", axis=1, tiled=False)
    shared_cat = shared_cat.reshape(width, 3 * shared_cols)
    group_rows = lax.all_gather(normed, "mp", axis=0, tiled=True)
    kv_cols = kv_weight.shape[1]
    kv_full = lax.all_to_all(
        jnp.broadcast_to(kv_weight[None], (n_mp,) + kv_weight.shape), "mp", 0, 0, tiled=True
    )
    received[0], shared_cat, group_rows, kv_full = lax.optimization_barrier(
        (received[0], shared_cat, group_rows, kv_full)
    )
    back = []
    for c, (lo, hi) in enumerate(spans):
        chunk = hi - lo
        slots_here = received[c].reshape(n_groups * chunk, width)
        rows = lax.all_gather(slots_here, "mp", axis=0, tiled=True)
        summed = lax.psum_scatter(
            expert_part(rows, gate_up_w, down_w).astype(jnp.bfloat16),
            "mp",
            scatter_dimension=0,
            tiled=True,
        )
        back.append(
            lax.all_to_all(
                summed.reshape(n_groups, chunk, width),
                ("dp", "expert"),
                split_axis=0,
                concat_axis=0,
                tiled=True,
            )
        )
    back = jnp.concatenate(back, axis=1).reshape(n_groups * capacity, width)
    slot_weight = jnp.sum(jnp.where(token_slot, gate_weights[:, :, None], 0.0), axis=1)
    routed = jnp.dot(
        slot_weight,
        back.astype(jnp.float32),
        precision=lax.Precision.HIGHEST,
        preferred_element_type=jnp.float32,
    )
    gate_w = shared_cat[:, :shared_cols]
    up_w = shared_cat[:, shared_cols : 2 * shared_cols]
    down_s = shared_cat[:, 2 * shared_cols :]
    rows = group_rows
    gate_part = jnp.dot(rows, gate_w, preferred_element_type=jnp.float32)
    up_part = jnp.dot(rows, up_w, preferred_element_type=jnp.float32)
    act = (jax.nn.silu(gate_part) * up_part).astype(jnp.bfloat16)
    shared_out = lax.psum_scatter(
        lax.dot_general(act, down_s, (((1,), (1,)), ((), ())), preferred_element_type=jnp.float32),
        "mp",
        scatter_dimension=0,
        tiled=True,
    )
    layer_out = (hidden.astype(jnp.float32) + routed + shared_out).astype(jnp.bfloat16)
    next_rows = rms_scale(layer_out, next_gain)
    kv_full = kv_full.transpose(1, 0, 2).reshape(width, n_mp * kv_cols)
    kv_local = jnp.dot(next_rows, kv_full, preferred_element_type=jnp.float32).astype(jnp.bfloat16)
    kv_send = kv_local.reshape(tok_rows, n_mp, kv_cols).transpose(1, 0, 2)
    kv_latent = lax.all_to_all(kv_send, "mp", 0, 0, tiled=True).reshape(n_mp * tok_rows, kv_cols)
    return (layer_out, kv_latent)


def solution(mesh):
    in_specs = (
        P(("dp", "expert", "mp"), None),
        P(),
        P("dp", ("expert", "mp"), None),
        P("dp", ("expert", "mp"), None),
        P(("dp", "expert", "mp"), None),
        P(("dp", "expert", "mp"), None),
        P(("dp", "expert"), "mp"),
        P(("dp", "expert"), "mp"),
        P(("dp", "expert"), "mp"),
        P(),
        P(None, "mp"),
    )
    out_specs = (P(("dp", "expert", "mp"), None), P(("dp", "expert"), "mp"))
    return jax.shard_map(
        on_device, mesh=mesh, in_specs=in_specs, out_specs=out_specs, check_vma=False
    )
```

profile of v0, /device:TPU:8, one launch (start us, length us, event | category | flops | bytes accessed | tf_op | source)
XLA Modules:
  0.0 541.9 jit_solution(3544073971727459353)
XLA Ops:
  7.2 1.1 fusion.31
  8.3 1.8 fusion.33
  10.2 1.0 concatenate.9
  11.2 21.2 %all-gather = bf16[128,2112]{1,0:T(8,128)(2,1)} all-gather(bf16[32,2112]{1,0:T(8,128)(2,1)S(1)} %concatenate.9), channel_id=2, replica_groups=mesh['dp'=4,'expert'=16,'mp'=4] {'dp'}, dimensions={0}, use_global_device_ids=true | all-gather | bytes 675840 | tf_op jit(solution)/shard_map/all_gather | solution.py:86
  32.5 0.8 copy.54
  33.5 0.9 reduce-window.6
  35.3 2.0 convolution_convert_fusion.2
  37.3 2.8 reshape.104
  40.1 2.1 slice.68
  42.2 42.6 %all_to_all.48 = bf16[64,4,2048]{2,1,0:T(4,128)(2,1)S(1)} all-to-all(bf16[64,4,2048]{2,1,0:T(4,128)(2,1)S(1)} %slice.68), channel_id=1, replica_groups=mesh['dp'=4,'expert'=16,'mp'=4] {'dp','expert'}, dimensions={0} | all-to-all | bytes 2097152 | tf_op jit(solution)/shard_map/all_to_all | solution.py:81
  84.8 1.1 reshape.113
  85.9 1.7 broadcast_in_dim.12
  87.6 4.3 all-to-all-start.1
  91.9 3.2 slice.61
  95.1 26.2 %all-to-all-done.1 = bf16[4,2048,144]{1,2,0:T(8,128)(2,1)S(1)} async-done(((bf16[4,2048,144]{1,2,0:T(8,128)(2,1)}), bf16[4,2048,144]{1,2,0:T(8,128)(2,1)S(1)}, u32[]{:S(2)}, u32[]{:S(2)}) %all-to-all-start.1) | async-done | bytes 2359328 | tf_op jit(solution)/shard_map/all_to_all | solution.py:91
  121.3 9.8 %all-to-all-start = ((bf16[64,8,2048]{2,1,0:T(8,128)(2,1)}), bf16[64,8,2048]{2,1,0:T(8,128)(2,1)}, u32[]{:S(2)}, u32[]{:S(2)}) async-start(bf16[64,8,2048]{2,1,0:T(8,128)(2,1)} %slice.61), calls=%async_computation | async-start | bytes 4194304 | tf_op jit(solution)/shard_map/all_to_all | solution.py:81
  131.2 51.1 %all-to-all-done = bf16[64,8,2048]{2,1,0:T(8,128)(2,1)} async-done(((bf16[64,8,2048]{2,1,0:T(8,128)(2,1)}), bf16[64,8,2048]{2,1,0:T(8,128)(2,1)}, u32[]{:S(2)}, u32[]{:S(2)}) %all-to-all-start) | async-done | bytes 2097184 | tf_op jit(solution)/shard_map/all_to_all | solution.py:81
  182.3 4.6 convert_element_type.61
  186.9 6.8 %reshape.107 = bf16[16,32,2,4,352]{4,3,2,1,0:T(4,128)(2,1)S(1)} reshape(bf16[16,32,2816]{2,1,0:T(8,128)(2,1)} %convert_element_type.61) | data formatting | bytes 5767168 | tf_op jit(solution)/shard_map/reshape | solution.py:45
  193.7 2.4 copy.58
  196.1 6.0 %all-to-all-start.2 = ((bf16[64,32,2,352]{3,1,2,0:T(8,128)(2,1)}), bf16[64,32,2,352]{3,1,2,0:T(8,128)(2,1)S(1)}, u32[]{:S(2)}, u32[]{:S(2)}) async-start(bf16[64,32,2,352]{3,1,2,0:T(8,128)(2,1)} %bitcast.48), calls=%async_computation.2 | async-start | bytes 6291456 | tf_op jit(solution)/shard_map/all_to_all | solution.py:56
  202.0 2.0 convert_element_type.63
  204.5 1.4 pad_maximum_fusion.1
  205.9 48.5 %all-to-all-done.2 = bf16[64,32,2,352]{3,1,2,0:T(8,128)(2,1)S(1)} async-done(((bf16[64,32,2,352]{3,1,2,0:T(8,128)(2,1)}), bf16[64,32,2,352]{3,1,2,0:T(8,128)(2,1)S(1)}, u32[]{:S(2)}, u32[]{:S(2)}) %all-to-all-start.2) | async-done | bytes 2883616 | tf_op jit(solution)/shard_map/all_to_all | solution.py:56
  254.4 9.1 %all-to-all-start.3 = ((bf16[64,32,352]{2,1,0:T(8,128)(2,1)}), bf16[64,32,352]{2,1,0:T(8,128)(2,1)}, u32[]{:S(2)}, u32[]{:S(2)}) async-start(bf16[64,32,352]{2,1,0:T(8,128)(2,1)} %bitcast.51), calls=%async_computation.3 | async-start | bytes 3145728 | tf_op jit(solution)/shard_map/all_to_all | solution.py:57
  264.0 4.9 copy.59
  268.9 6.4 %reshape.109 = bf16[2048,704]{1,0:T(8,128)(2,1)S(1)} reshape(bf16[64,32,2,352]{3,2,1,0:T(2,128)(2,1)} %copy.59) | data formatting | bytes 5767168 | tf_op jit(solution)/shard_map/reshape | solution.py:59
  275.4 7.0 %fusion.47 = f32[1024,704]{0,1:T(8,128)} fusion(bf16[1024,2048]{1,0:T(8,128)(2,1)} %all-gather.11.cloned.1.call-done, bf16[2048,704]{1,0:T(8,128)(2,1)S(1)} %reshape.109), kind=kOutput, calls=%fused_computation.64 | convolution fusion | flops 2952790016 | bytes 9961472 | tf_op jit(solution)/shard_map/dot_general | solution.py:15
  282.4 10.2 %all-to-all-done.3 = bf16[64,32,352]{2,1,0:T(8,128)(2,1)} async-done(((bf16[64,32,352]{2,1,0:T(8,128)(2,1)}), bf16[64,32,352]{2,1,0:T(8,128)(2,1)}, u32[]{:S(2)}, u32[]{:S(2)}) %all-to-all-start.3) | async-done | bytes 1441824 | tf_op jit(solution)/shard_map/all_to_all | solution.py:57
  292.6 6.7 %convolution_convert_fusion.1 = bf16[1024,2048]{1,0:T(8,128)(2,1)} fusion(bf16[2048,352]{1,0:T(8,128)(2,1)} %bitcast.7, f32[1024,704]{0,1:T(8,128)} %fusion.47), kind=kOutput, calls=%fused_computation.2 | convolution fusion | flops 1480654848 | bytes 8519680 | tf_op jit(solution)/shard_map/dot_general | solution.py:17
  299.6 13.5 %all-gather.9.cloned.1.call-done = bf16[2048,2048]{1,0:T(8,128)(2,1)} async-done(((bf16[512,2048]{1,0:T(8,128)(2,1)}), bf16[2048,2048]{1,0:T(8,128)(2,1)}) %all-gather.9.cloned.1.call-update) | async-done | bytes 8388624 | tf_op jit(solution)/shard_map/all_gather | solution.py:101
  313.0 8.8 %fusion.46 = f32[2048,704]{0,1:T(8,128)S(1)} fusion(bf16[2048,2048]{1,0:T(8,128)(2,1)} %all-gather.9.cloned.1.call-done, bf16[2048,704]{1,0:T(8,128)(2,1)S(1)} %reshape.109), kind=kOutput, calls=%fused_computation.63 | convolution fusion | flops 5905580032 | bytes 17039360 | tf_op jit(solution)/shard_map/dot_general | solution.py:15
  321.9 8.3 %convolution_convert_fusion = bf16[2048,2048]{1,0:T(8,128)(2,1)} fusion(bf16[2048,352]{1,0:T(8,128)(2,1)} %bitcast.7, f32[2048,704]{0,1:T(8,128)S(1)} %fusion.46), kind=kOutput, calls=%fused_computation | convolution fusion | flops 2961309696 | bytes 15597568 | tf_op jit(solution)/shard_map/dot_general | solution.py:17
  330.2 35.6 %reduce-scatter.6.cloned.1.call-done = bf16[256,2048]{1,0:T(8,128)(2,1)} async-done(((bf16[1024,2048]{1,0:T(8,128)(2,1)}), bf16[256,2048]{1,0:T(8,128)(2,1)}) %reduce-scatter.6.cloned.1.call-update) | async-done | bytes 1048592 | tf_op jit(solution)/shard_map/reduce_scatter | solution.py:102
  365.8 2.2 reshape.114
  368.0 10.6 %all-to-all-start.6 = ((bf16[64,4,2048]{2,1,0:T(4,128)(2,1)}), bf16[64,4,2048]{2,1,0:T(4,128)(2,1)S(1)}, u32[]{:S(2)}, u32[]{:S(2)}) async-start(bf16[64,4,2048]{2,1,0:T(4,128)(2,1)} %reshape.114), calls=%async_computation.8 | async-start | bytes 2097152 | tf_op jit(solution)/shard_map/all_to_all | solution.py:109
  378.6 4.8 fusion.4
  383.4 24.0 %all-to-all-done.6 = bf16[64,4,2048]{2,1,0:T(4,128)(2,1)S(1)} async-done(((bf16[64,4,2048]{2,1,0:T(4,128)(2,1)}), bf16[64,4,2048]{2,1,0:T(4,128)(2,1)S(1)}, u32[]{:S(2)}, u32[]{:S(2)}) %all-to-all-start.6) | async-done | bytes 1048608 | tf_op jit(solution)/shard_map/all_to_all | solution.py:109
  407.4 43.8 %reduce-scatter.4.cloned.1.call-done = bf16[512,2048]{1,0:T(8,128)(2,1)} async-done(((bf16[2048,2048]{1,0:T(8,128)(2,1)}), bf16[512,2048]{1,0:T(8,128)(2,1)}) %reduce-scatter.4.cloned.1.call-update) | async-done | bytes 2097168 | tf_op jit(solution)/shard_map/reduce_scatter | solution.py:102
  451.2 10.6 %all-to-all-start.4 = ((bf16[64,8,2048]{2,1,0:T(8,128)(2,1)}), bf16[64,8,2048]{2,1,0:T(8,128)(2,1)S(1)}, u32[]{:S(2)}, u32[]{:S(2)}) async-start(bf16[64,8,2048]{2,1,0:T(8,128)(2,1)} %bitcast.53), calls=%async_computation.5 | async-start | bytes 4194304 | tf_op jit(solution)/shard_map/all_to_all | solution.py:109
  462.1 9.2 %fusion = f32[256,2048]{1,0:T(8,128)} fusion(bf16[2048,2112]{1,0:T(8,128)(2,1)} %bitcast.58, bf16[256,2048]{1,0:T(8,128)(2,1)} %all-gather.7.cloned.1.call-done, f32[256,704]{0,1:T(8,128)} %fusion.4), kind=kOutput, calls=%fused_computation.4 | convolution fusion | flops 1477476352 | bytes 10158080 | tf_op jit(solution)/shard_map/dot_general | solution.py:133
  471.4 0.9 select_reduce_fusion
  472.3 40.8 %all-to-all-done.4 = bf16[64,8,2048]{2,1,0:T(8,128)(2,1)S(1)} async-done(((bf16[64,8,2048]{2,1,0:T(8,128)(2,1)}), bf16[64,8,2048]{2,1,0:T(8,128)(2,1)S(1)}, u32[]{:S(2)}, u32[]{:S(2)}) %all-to-all-start.4) | async-done | bytes 2097184 | tf_op jit(solution)/shard_map/all_to_all | solution.py:109
  513.1 2.7 pad_maximum_fusion
  515.8 4.8 reshape.115
  520.6 3.2 fusion.28
  524.5 0.8 convolution_convert_fusion.3
  525.5 8.5 %all_to_all.49 = bf16[4,64,144]{2,1,0:T(8,128)(2,1)S(1)} all-to-all(bf16[4,64,144]{2,1,0:T(8,128)(2,1)S(1)} %bitcast.54), channel_id=1, replica_groups=mesh['dp'=4,'expert'=16,'mp'=4] {'mp'}, dimensions={0} | all-to-all | bytes 147456 | tf_op jit(solution)/shard_map/all_to_all | solution.py:143
  (54 shorter events, 4.6 us)
Async XLA Ops:
  7.2 27.9 %copy-start.5 = (s32[64,6]{0,1:T(8,128)S(1)}, s32[64,6]{0,1:T(8,128)}, u32[]{:S(2)}) copy-start(s32[64,6]{0,1:T(8,128)} %param.15) | copy-start | bytes 4612
  7.2 124.0 %all-gather.7.cloned.1.call-start = ((), (), s32[]{:S(2)}) async-start(), calls=%async_computation.11 | async-start | bytes 1310720 | tf_op jit(solution)/shard_map/all_gather | solution.py:89
  10.2 172.1 %all-gather.13.cloned.1.call-start = ((), (), s32[]{:S(2)}) async-start(), calls=%async_computation.17 | async-start | bytes 9469952 | tf_op jit(solution)/shard_map/all_gather | solution.py:87
  32.4 243.0 %all-gather.11.cloned.1.call-start = ((), (), s32[]{:S(2)}) async-start(), calls=%async_computation.14 | async-start | bytes 5242880 | tf_op jit(solution)/shard_map/all_gather | solution.py:101
  42.2 43.7 %copy-start.4 = (bf16[2048,144]{0,1:T(8,128)(2,1)S(1)}, bf16[2048,144]{0,1:T(8,128)(2,1)}, u32[]{:S(2)}) copy-start(bf16[2048,144]{0,1:T(8,128)(2,1)} %param.21) | copy-start | bytes 1769476
  87.6 33.7 %all-to-all-start.1 = ((bf16[4,2048,144]{1,2,0:T(8,128)(2,1)}), bf16[4,2048,144]{1,2,0:T(8,128)(2,1)S(1)}, u32[]{:S(2)}, u32[]{:S(2)}) async-start(bf16[4,2048,144]{1,2,0:T(8,128)(2,1)} %broadcast_in_dim.12), calls=%async_computation.1 | async-start | bytes 4718592 | tf_op jit(solution)/shard_map/all_to_all | solution.py:91
  121.3 61.0 %copy-start = (bf16[4,2048,144]{1,2,0:T(8,128)(2,1)}, bf16[4,2048,144]{1,2,0:T(8,128)(2,1)S(1)}, u32[]{:S(2)}) copy-start(bf16[4,2048,144]{1,2,0:T(8,128)(2,1)S(1)} %all-to-all-done.1) | copy-start | bytes 7077892
  121.3 61.0 %all-to-all-start = ((bf16[64,8,2048]{2,1,0:T(8,128)(2,1)}), bf16[64,8,2048]{2,1,0:T(8,128)(2,1)}, u32[]{:S(2)}, u32[]{:S(2)}) async-start(bf16[64,8,2048]{2,1,0:T(8,128)(2,1)} %slice.61), calls=%async_computation | async-start | bytes 4194304 | tf_op jit(solution)/shard_map/all_to_all | solution.py:81
  131.1 181.9 %all-gather.9.cloned.1.call-start = ((), (), s32[]{:S(2)}) async-start(), calls=%async_computation.12 | async-start | bytes 10485760 | tf_op jit(solution)/shard_map/all_gather | solution.py:101
  196.1 58.3 %all-to-all-start.2 = ((bf16[64,32,2,352]{3,1,2,0:T(8,128)(2,1)}), bf16[64,32,2,352]{3,1,2,0:T(8,128)(2,1)S(1)}, u32[]{:S(2)}, u32[]{:S(2)}) async-start(bf16[64,32,2,352]{3,1,2,0:T(8,128)(2,1)} %bitcast.48), calls=%async_computation.2 | async-start | bytes 6291456 | tf_op jit(solution)/shard_map/all_to_all | solution.py:56
  254.4 38.2 %all-to-all-start.3 = ((bf16[64,32,352]{2,1,0:T(8,128)(2,1)}), bf16[64,32,352]{2,1,0:T(8,128)(2,1)}, u32[]{:S(2)}, u32[]{:S(2)}) async-start(bf16[64,32,352]{2,1,0:T(8,128)(2,1)} %bitcast.51), calls=%async_computation.3 | async-start | bytes 3145728 | tf_op jit(solution)/shard_map/all_to_all | solution.py:57
  263.5 102.3 %reduce-scatter.6.cloned.1.call-start = ((), (), s32[]{:S(2)}) async-start(), calls=%async_computation.15 | async-start | bytes 5242880 | tf_op jit(solution)/shard_map/reduce_scatter | solution.py:102
  299.3 151.9 %reduce-scatter.4.cloned.1.call-start = ((), (), s32[]{:S(2)}) async-start(), calls=%async_computation.13 | async-start | bytes 10485760 | tf_op jit(solution)/shard_map/reduce_scatter | solution.py:102
  330.2 48.4 %copy-start.8 = (bf16[256,2048]{1,0:T(8,128)(2,1)S(1)}, bf16[256,2048]{1,0:T(8,128)(2,1)}, u32[]{:S(2)}) copy-start(bf16[256,2048]{1,0:T(8,128)(2,1)} %all-gather.7.cloned.1.call-done) | copy-start | bytes 3145732
  368.0 39.4 %all-to-all-start.6 = ((bf16[64,4,2048]{2,1,0:T(4,128)(2,1)}), bf16[64,4,2048]{2,1,0:T(4,128)(2,1)S(1)}, u32[]{:S(2)}, u32[]{:S(2)}) async-start(bf16[64,4,2048]{2,1,0:T(4,128)(2,1)} %reshape.114), calls=%async_computation.8 | async-start | bytes 2097152 | tf_op jit(solution)/shard_map/all_to_all | solution.py:109
  451.2 61.8 %all-to-all-start.4 = ((bf16[64,8,2048]{2,1,0:T(8,128)(2,1)}), bf16[64,8,2048]{2,1,0:T(8,128)(2,1)S(1)}, u32[]{:S(2)}, u32[]{:S(2)}) async-start(bf16[64,8,2048]{2,1,0:T(8,128)(2,1)} %bitcast.53), calls=%async_computation.5 | async-start | bytes 4194304 | tf_op jit(solution)/shard_map/all_to_all | solution.py:109
  461.8 9.5 %copy-start.6 = (s32[64,6]{0,1:T(8,128)S(1)}, s32[64,6]{0,1:T(8,128)}, u32[]{:S(2)}) copy-start(s32[64,6]{0,1:T(8,128)} %param.16) | copy-start | bytes 4612
  461.8 58.8 %reduce-scatter.8.cloned.1.call-start = ((), (), s32[]{:S(2)}) async-start(), calls=%async_computation.16 | async-start | bytes 2621440 | tf_op jit(solution)/shard_map/reduce_scatter | solution.py:132
  515.8 4.8 copy-start.2
  520.6 3.9 copy-start.7
  520.6 3.9 copy-start.1
  523.8 0.7 copy-start.3
Sparse Core Ops, SparseCore 0:
  10.4 29.3 all-gather.6
  41.6 74.7 all-gather.12
  118.2 53.2 all-gather.10
  182.4 130.5 all-gather.8
  315.4 50.3 reduce-scatter.5
  368.4 82.7 reduce-scatter.3
  471.5 31.7 reduce-scatter.7
where the time goes:
time: 551 us; the launch traced here: 542 us
  waiting for transfers between devices  294 us (53%)
  blocking collectives  72.3 us (13%)
  starting transfers between devices  51.4 us (9%)
  matrix products  50.9 us (9%)
  local copies, waits for them, and re-layouts  42.9 us (8%)
  other arithmetic  15.9 us (3%)
  between operations  14.7 us (3%)
    reduce_scatter x2, waiting for transfers between devices, on_device(): lax.psum_scatter(expert_part(rows, gate_up_w, down_w).astype(jnp.bfloat16...  79.4 us
    all_to_all x2, waiting for transfers between devices, on_device(): lax.all_to_all(summed.reshape(n_groups, chunk, width), ('dp', 'expert'),...  64.8 us
    all_to_all x1, waiting for transfers between devices, on_device(): lax.all_to_all(send[:, lo:hi], ('dp', 'expert'), split_axis=0, concat_axi...  51.1 us
    all_to_all x1, waiting for transfers between devices, on_device(): lax.all_to_all(in_send, ('expert', 'mp'), split_axis=0, concat_axis=1, ti...  48.5 us
    all_to_all x1, blocking collectives, on_device(): lax.all_to_all(send[:, lo:hi], ('dp', 'expert'), split_axis=0, concat_axi...  42.6 us
    all_to_all x1, waiting for transfers between devices, on_device(): lax.all_to_all(jnp.broadcast_to(kv_weight[None], (n_mp,) + kv_weight.shap...  26.2 us
    all_gather x1, blocking collectives, on_device(): shared_cat = lax.all_gather(shared_cat, 'dp', axis=0, tiled=False)  21.2 us
    all_to_all x2, starting transfers between devices, on_device(): lax.all_to_all(summed.reshape(n_groups, chunk, width), ('dp', 'expert'),...  21.1 us
  transfers between devices with their start and end apart: 13, of which 9 were waited for; matrix products, arithmetic and copies ran while one was open for 19% of the time, Pallas kernels for 0%

commit v1 on v0

--- a/solution.py
+++ b/solution.py
@@ -98,7 +98,9 @@
     for c, (lo, hi) in enumerate(spans):
         chunk = hi - lo
         slots_here = received[c].reshape(n_groups * chunk, width)
-        rows = lax.all_gather(slots_here, "mp", axis=0, tiled=True)
+        rows = jnp.concatenate(
+            lax.all_to_all(jnp.stack([slots_here] * lax.axis_size("mp")), "mp", 0, 0), axis=0
+        )
         summed = lax.psum_scatter(
             expert_part(rows, gate_up_w, down_w).astype(jnp.bfloat16),
             "mp",

time: 551 us -> 653 us (1.19)
  waiting for transfers between devices: 294 us -> 398 us
  blocking collectives: 72.3 us -> 46.3 us
  starting transfers between devices: 51.4 us -> 69.9 us
  local copies, waits for them, and re-layouts: 42.9 us -> 54.1 us
    all_to_all x0 -> x2, waiting for transfers between devices: none -> 156 us  [on_device(): lax.all_to_all(jnp.stack([slots_here] * lax.axis_size('mp')), 'mp', 0, 0)]
    all_to_all x1 -> x0, blocking collectives: 42.6 us -> none  [on_device(): lax.all_to_all(send[:, lo:hi], ('dp', 'expert'), split_axis=0, concat_axi...]
    reduce_scatter x2, waiting for transfers between devices: 79.4 us -> 40.9 us  [on_device(): lax.psum_scatter(expert_part(rows, gate_up_w, down_w).astype(jnp.bfloat16...]
    all_gather x1, blocking collectives: 21.2 us -> 37.8 us  [on_device(): shared_cat = lax.all_gather(shared_cat, 'dp', axis=0, tiled=False)]
    all_to_all x1, waiting for transfers between devices: 10.2 us -> 25.9 us  [on_device(): lax.all_to_all(out_send, ('expert', 'mp'), split_axis=0, concat_axis=1, t...]
    all_gather x2 -> x0, waiting for transfers between devices: 13.5 us -> none  [on_device(): rows = lax.all_gather(slots_here, 'mp', axis=0, tiled=True)]
    all_to_all x1, waiting for transfers between devices: 48.5 us -> 36.3 us  [on_device(): lax.all_to_all(in_send, ('expert', 'mp'), split_axis=0, concat_axis=1, ti...]
    another operation x1 -> x4, local copies, waits for them, and re-layouts: 0.48 us -> 12.3 us  [the longest x3 11.9 us: on_device(): jnp.stack([slots_here] * lax.axis_size('mp'))]
  transfers between devices with their start and end apart: 13 -> 14, of which waited for: 9 -> 9; matrix products, arithmetic and copies ran while one was open for 19% -> 15% of each run, Pallas kernels for 0% -> 0%
where the time goes in v1:
time: 653 us; the launch traced here: 644 us
  waiting for transfers between devices  398 us (61%)
  starting transfers between devices  69.9 us (11%)
  local copies, waits for them, and re-layouts  54.1 us (8%)
  matrix products  46.3 us (7%)
  blocking collectives  46.3 us (7%)
  between operations  14.4 us (2%)
  other arithmetic  14 us (2%)
    all_to_all x2, waiting for transfers between devices, on_device(): lax.all_to_all(jnp.stack([slots_here] * lax.axis_size('mp')), 'mp', 0, 0)  156 us
    all_to_all x2, waiting for transfers between devices, on_device(): lax.all_to_all(summed.reshape(n_groups, chunk, width), ('dp', 'expert'),...  65.6 us
    all_to_all x2, waiting for transfers between devices, on_device(): lax.all_to_all(send[:, lo:hi], ('dp', 'expert'), split_axis=0, concat_axi...  54.8 us
    reduce_scatter x2, waiting for transfers between devices, on_device(): lax.psum_scatter(expert_part(rows, gate_up_w, down_w).astype(jnp.bfloat16...  40.9 us
    all_gather x1, blocking collectives, on_device(): shared_cat = lax.all_gather(shared_cat, 'dp', axis=0, tiled=False)  37.8 us
    all_to_all x1, waiting for transfers between devices, on_device(): lax.all_to_all(in_send, ('expert', 'mp'), split_axis=0, concat_axis=1, ti...  36.3 us
    all_to_all x1, waiting for transfers between devices, on_device(): lax.all_to_all(out_send, ('expert', 'mp'), split_axis=0, concat_axis=1, t...  25.9 us
    all_to_all x2, starting transfers between devices, on_device(): lax.all_to_all(send[:, lo:hi], ('dp', 'expert'), split_axis=0, concat_axi...  21 us
  transfers between devices with their start and end apart: 14, of which 9 were waited for; matrix products, arithmetic and copies ran while one was open for 15% of the time, Pallas kernels for 0%

profile of v1, /device:TPU:8, one launch (start us, length us, event | category | flops | bytes accessed | tf_op | source)
XLA Modules:
  0.0 643.6 jit_solution(10284468769924234417)
XLA Ops:
  7.2 2.8 broadcast_in_dim.12
  10.0 4.6 all-to-all-start.1
  15.0 0.9 reduce-window.6
  17.8 2.0 convolution_convert_fusion.2
  19.8 2.7 reshape.108
  22.5 3.2 slice.68
  25.7 18.4 %all-to-all-done.1 = bf16[4,2048,144]{1,2,0:T(8,128)(2,1)} async-done(((bf16[4,2048,144]{1,2,0:T(8,128)(2,1)}), bf16[4,2048,144]{1,2,0:T(8,128)(2,1)}, u32[]{:S(2)}, u32[]{:S(2)}) %all-to-all-start.1) | async-done | bytes 2359328 | tf_op jit(solution)/shard_map/all_to_all | solution.py:91
  44.1 12.1 %all-to-all-start.6 = ((bf16[64,4,2048]{2,1,0:T(4,128)(2,1)}), bf16[64,4,2048]{2,1,0:T(4,128)(2,1)S(1)}, u32[]{:S(2)}, u32[]{:S(2)}) async-start(bf16[64,4,2048]{2,1,0:T(4,128)(2,1)} %slice.68), calls=%async_computation.7 | async-start | bytes 2097152 | tf_op jit(solution)/shard_map/all_to_all | solution.py:81
  57.1 37.8 %all-gather = bf16[128,2112]{1,0:T(8,128)(2,1)} all-gather(bf16[32,2112]{1,0:T(8,128)(2,1)S(1)} %concatenate.9), channel_id=2, replica_groups=mesh['dp'=4,'expert'=16,'mp'=4] {'dp'}, dimensions={0}, use_global_device_ids=true | all-gather | bytes 675840 | tf_op jit(solution)/shard_map/all_gather | solution.py:86
  95.0 2.0 convert_element_type.63
  97.4 1.4 pad_maximum_fusion.1
  98.8 5.8 all-to-all-start.4
  104.6 3.1 slice.61
  107.8 25.9 %all-to-all-done.4 = bf16[64,32,352]{2,1,0:T(8,128)(2,1)S(1)} async-done(((bf16[64,32,352]{2,1,0:T(8,128)(2,1)}), bf16[64,32,352]{2,1,0:T(8,128)(2,1)S(1)}, u32[]{:S(2)}, u32[]{:S(2)}) %all-to-all-start.4) | async-done | bytes 1441824 | tf_op jit(solution)/shard_map/all_to_all | solution.py:57
  133.7 8.9 %all-to-all-start = ((bf16[64,8,2048]{2,1,0:T(8,128)(2,1)}), bf16[64,8,2048]{2,1,0:T(8,128)(2,1)}, u32[]{:S(2)}, u32[]{:S(2)}) async-start(bf16[64,8,2048]{2,1,0:T(8,128)(2,1)} %slice.61), calls=%async_computation | async-start | bytes 4194304 | tf_op jit(solution)/shard_map/all_to_all | solution.py:81
  142.7 4.7 convert_element_type.61
  147.3 6.6 %reshape.111 = bf16[16,32,2,4,352]{4,3,2,1,0:T(4,128)(2,1)S(1)} reshape(bf16[16,32,2816]{2,1,0:T(8,128)(2,1)} %convert_element_type.61) | data formatting | bytes 5767168 | tf_op jit(solution)/shard_map/reshape | solution.py:45
  154.0 2.4 copy.58
  156.3 54.8 %all-to-all-done = bf16[64,8,2048]{2,1,0:T(8,128)(2,1)} async-done(((bf16[64,8,2048]{2,1,0:T(8,128)(2,1)}), bf16[64,8,2048]{2,1,0:T(8,128)(2,1)}, u32[]{:S(2)}, u32[]{:S(2)}) %all-to-all-start) | async-done | bytes 2097184 | tf_op jit(solution)/shard_map/all_to_all | solution.py:81
  211.1 9.2 %all-to-all-start.3 = ((bf16[64,32,2,352]{3,1,2,0:T(8,128)(2,1)}), bf16[64,32,2,352]{3,1,2,0:T(8,128)(2,1)S(1)}, u32[]{:S(2)}, u32[]{:S(2)}) async-start(bf16[64,32,2,352]{3,1,2,0:T(8,128)(2,1)} %bitcast.50), calls=%async_computation.3 | async-start | bytes 6291456 | tf_op jit(solution)/shard_map/all_to_all | solution.py:56
  220.3 2.1 stack_reshape.5
  222.5 36.3 %all-to-all-done.3 = bf16[64,32,2,352]{3,1,2,0:T(8,128)(2,1)S(1)} async-done(((bf16[64,32,2,352]{3,1,2,0:T(8,128)(2,1)}), bf16[64,32,2,352]{3,1,2,0:T(8,128)(2,1)S(1)}, u32[]{:S(2)}, u32[]{:S(2)}) %all-to-all-start.3) | async-done | bytes 2883616 | tf_op jit(solution)/shard_map/all_to_all | solution.py:56
  258.8 3.8 stack.7
  262.6 5.3 all-to-all-start.7
  267.9 4.9 copy.59
  272.8 6.4 %reshape.113 = bf16[2048,704]{1,0:T(8,128)(2,1)S(1)} reshape(bf16[64,32,2,352]{3,2,1,0:T(2,128)(2,1)} %copy.59) | data formatting | bytes 5767168 | tf_op jit(solution)/shard_map/reshape | solution.py:59
  279.3 38.2 %all-to-all-done.7 = bf16[4,256,2048]{2,1,0:T(8,128)(2,1)} async-done(((bf16[4,256,2048]{2,1,0:T(8,128)(2,1)}), bf16[4,256,2048]{2,1,0:T(8,128)(2,1)}, u32[]{:S(2)}, u32[]{:S(2)}) %all-to-all-start.7) | async-done | bytes 4194336 | tf_op jit(solution)/shard_map/all_to_all | solution.py:102
  317.5 5.9 stack.6
  323.5 5.7 all-to-all-start.2
  329.2 5.1 fusion.47
  334.3 4.5 convolution_convert_fusion.1
  339.1 117.5 %all-to-all-done.2 = bf16[4,512,2048]{2,1,0:T(8,128)(2,1)} async-done(((bf16[4,512,2048]{2,1,0:T(8,128)(2,1)}), bf16[4,512,2048]{2,1,0:T(8,128)(2,1)}, u32[]{:S(2)}, u32[]{:S(2)}) %all-to-all-start.2) | async-done | bytes 8388640 | tf_op jit(solution)/shard_map/all_to_all | solution.py:102
  456.6 8.9 %fusion.46 = f32[2048,704]{0,1:T(8,128)S(1)} fusion(bf16[2048,2048]{1,0:T(8,128)(2,1)} %bitcast.4, bf16[2048,704]{1,0:T(8,128)(2,1)S(1)} %reshape.113), kind=kOutput, calls=%fused_computation.63 | convolution fusion | flops 5905580032 | bytes 17039360 | tf_op jit(solution)/shard_map/dot_general | solution.py:15
  465.6 7.0 %convolution_convert_fusion = bf16[2048,2048]{1,0:T(8,128)(2,1)} fusion(bf16[2048,352]{1,0:T(8,128)(2,1)S(1)} %bitcast.55, f32[2048,704]{0,1:T(8,128)S(1)} %fusion.46), kind=kOutput, calls=%fused_computation | convolution fusion | flops 2961309696 | bytes 15597568 | tf_op jit(solution)/shard_map/dot_general | solution.py:17
  472.7 2.4 reshape.118
  475.0 7.1 %all-to-all-start.8 = ((bf16[64,4,2048]{2,1,0:T(4,128)(2,1)}), bf16[64,4,2048]{2,1,0:T(4,128)(2,1)S(1)}, u32[]{:S(2)}, u32[]{:S(2)}) async-start(bf16[64,4,2048]{2,1,0:T(4,128)(2,1)} %reshape.118), calls=%async_computation.10 | async-start | bytes 2097152 | tf_op jit(solution)/shard_map/all_to_all | solution.py:111
  482.1 4.1 fusion.4
  486.2 24.7 %all-to-all-done.8 = bf16[64,4,2048]{2,1,0:T(4,128)(2,1)S(1)} async-done(((bf16[64,4,2048]{2,1,0:T(4,128)(2,1)}), bf16[64,4,2048]{2,1,0:T(4,128)(2,1)S(1)}, u32[]{:S(2)}, u32[]{:S(2)}) %all-to-all-start.8) | async-done | bytes 1048608 | tf_op jit(solution)/shard_map/all_to_all | solution.py:111
  510.9 40.9 %reduce-scatter.4.cloned.1.call-done = bf16[512,2048]{1,0:T(8,128)(2,1)} async-done(((bf16[2048,2048]{1,0:T(8,128)(2,1)}), bf16[512,2048]{1,0:T(8,128)(2,1)}) %reduce-scatter.4.cloned.1.call-update) | async-done | bytes 2097168 | tf_op jit(solution)/shard_map/reduce_scatter | solution.py:104
  551.8 10.6 %all-to-all-start.5 = ((bf16[64,8,2048]{2,1,0:T(8,128)(2,1)}), bf16[64,8,2048]{2,1,0:T(8,128)(2,1)S(1)}, u32[]{:S(2)}, u32[]{:S(2)}) async-start(bf16[64,8,2048]{2,1,0:T(8,128)(2,1)} %bitcast.53), calls=%async_computation.6 | async-start | bytes 4194304 | tf_op jit(solution)/shard_map/all_to_all | solution.py:111
  562.7 9.2 %fusion = f32[256,2048]{1,0:T(8,128)} fusion(bf16[2048,2112]{1,0:T(8,128)(2,1)} %bitcast.60, bf16[256,2048]{1,0:T(8,128)(2,1)} %all-gather.5.cloned.1.call-done, f32[256,704]{0,1:T(8,128)} %fusion.4), kind=kOutput, calls=%fused_computation.4 | convolution fusion | flops 1477476352 | bytes 10158080 | tf_op jit(solution)/shard_map/dot_general | solution.py:135
  571.9 0.9 select_reduce_fusion
  572.8 40.9 %all-to-all-done.5 = bf16[64,8,2048]{2,1,0:T(8,128)(2,1)S(1)} async-done(((bf16[64,8,2048]{2,1,0:T(8,128)(2,1)}), bf16[64,8,2048]{2,1,0:T(8,128)(2,1)S(1)}, u32[]{:S(2)}, u32[]{:S(2)}) %all-to-all-start.5) | async-done | bytes 2097184 | tf_op jit(solution)/shard_map/all_to_all | solution.py:111
  613.7 2.7 pad_maximum_fusion
  616.4 4.7 reshape.119
  621.2 3.0 fusion.28
  624.9 2.5 convolution_convert_fusion.3
  627.6 8.5 %all_to_all.58 = bf16[4,64,144]{2,1,0:T(8,128)(2,1)S(1)} all-to-all(bf16[4,64,144]{2,1,0:T(8,128)(2,1)S(1)} %bitcast.56), channel_id=1, replica_groups=mesh['dp'=4,'expert'=16,'mp'=4] {'mp'}, dimensions={0} | all-to-all | bytes 147456 | tf_op jit(solution)/shard_map/all_to_all | solution.py:145
  (65 shorter events, 5.9 us)
Async XLA Ops:
  7.2 7.4 %copy-start.9 = (s32[64,6]{0,1:T(8,128)S(1)}, s32[64,6]{0,1:T(8,128)}, u32[]{:S(2)}) copy-start(s32[64,6]{0,1:T(8,128)} %param.15) | copy-start | bytes 4612
  10.0 6.8 %copy-start.1 = (bf16[64,2048]{1,0:T(8,128)(2,1)S(1)}, bf16[64,2048]{1,0:T(8,128)(2,1)}, u32[]{:S(2)}) copy-start(bf16[64,2048]{1,0:T(8,128)(2,1)} %param.11) | copy-start | bytes 786436
  10.0 7.0 %copy-start.11 = (f32[2048]{0:T(1024)S(1)}, f32[2048]{0:T(1024)}, u32[]{:S(2)}) copy-start(f32[2048]{0:T(1024)} %param.12) | copy-start | bytes 24580
  10.0 34.1 %all-to-all-start.1 = ((bf16[4,2048,144]{1,2,0:T(8,128)(2,1)}), bf16[4,2048,144]{1,2,0:T(8,128)(2,1)}, u32[]{:S(2)}, u32[]{:S(2)}) async-start(bf16[4,2048,144]{1,2,0:T(8,128)(2,1)} %broadcast_in_dim.12), calls=%async_computation.1 | async-start | bytes 4718592 | tf_op jit(solution)/shard_map/all_to_all | solution.py:91
  22.5 34.5 %copy-start.6 = (bf16[32,704]{1,0:T(8,128)(2,1)S(1)}, bf16[32,704]{1,0:T(8,128)(2,1)}, u32[]{:S(2)}) copy-start(bf16[32,704]{1,0:T(8,128)(2,1)} %param.17) | copy-start | bytes 135172
  22.5 34.5 %copy-start.7 = (bf16[32,704]{1,0:T(8,128)(2,1)S(1)}, bf16[32,704]{1,0:T(8,128)(2,1)}, u32[]{:S(2)}) copy-start(bf16[32,704]{1,0:T(8,128)(2,1)} %param.18) | copy-start | bytes 135172
  22.5 34.5 %copy-start.8 = (bf16[32,704]{1,0:T(8,128)(2,1)S(1)}, bf16[32,704]{1,0:T(8,128)(2,1)}, u32[]{:S(2)}) copy-start(bf16[32,704]{1,0:T(8,128)(2,1)} %param.19) | copy-start | bytes 135172
  44.1 54.7 %all-to-all-start.6 = ((bf16[64,4,2048]{2,1,0:T(4,128)(2,1)}), bf16[64,4,2048]{2,1,0:T(4,128)(2,1)S(1)}, u32[]{:S(2)}, u32[]{:S(2)}) async-start(bf16[64,4,2048]{2,1,0:T(4,128)(2,1)} %slice.68), calls=%async_computation.7 | async-start | bytes 2097152 | tf_op jit(solution)/shard_map/all_to_all | solution.py:81
  56.2 223.1 %all-gather.5.cloned.1.call-start = ((), (), s32[]{:S(2)}) async-start(), calls=%async_computation.13 | async-start | bytes 1310720 | tf_op jit(solution)/shard_map/all_gather | solution.py:89
  56.9 222.4 %all-gather.7.cloned.1.call-start = ((), (), s32[]{:S(2)}) async-start(), calls=%async_computation.17 | async-start | bytes 9469952 | tf_op jit(solution)/shard_map/all_gather | solution.py:87
  98.8 9.0 %copy-start = (bf16[64,4,2048]{2,1,0:T(4,128)(2,1)}, bf16[64,4,2048]{2,1,0:T(4,128)(2,1)S(1)}, u32[]{:S(2)}) copy-start(bf16[64,4,2048]{2,1,0:T(4,128)(2,1)S(1)} %all-to-all-done.6) | copy-start | bytes 3145732
  98.8 34.9 %all-to-all-start.4 = ((bf16[64,32,352]{2,1,0:T(8,128)(2,1)}), bf16[64,32,352]{2,1,0:T(8,128)(2,1)S(1)}, u32[]{:S(2)}, u32[]{:S(2)}) async-start(bf16[64,32,352]{2,1,0:T(8,128)(2,1)} %bitcast.7), calls=%async_computation.4 | async-start | bytes 3145728 | tf_op jit(solution)/shard_map/all_to_all | solution.py:57
  133.7 8.9 %copy-start.2 = (bf16[64,32,352]{2,1,0:T(8,128)(2,1)}, bf16[64,32,352]{2,1,0:T(8,128)(2,1)S(1)}, u32[]{:S(2)}) copy-start(bf16[64,32,352]{2,1,0:T(8,128)(2,1)S(1)} %all-to-all-done.4) | copy-start | bytes 4325380
  133.7 77.4 %all-to-all-start = ((bf16[64,8,2048]{2,1,0:T(8,128)(2,1)}), bf16[64,8,2048]{2,1,0:T(8,128)(2,1)}, u32[]{:S(2)}, u32[]{:S(2)}) async-start(bf16[64,8,2048]{2,1,0:T(8,128)(2,1)} %slice.61), calls=%async_computation | async-start | bytes 4194304 | tf_op jit(solution)/shard_map/all_to_all | solution.py:81
  211.1 47.7 %all-to-all-start.3 = ((bf16[64,32,2,352]{3,1,2,0:T(8,128)(2,1)}), bf16[64,32,2,352]{3,1,2,0:T(8,128)(2,1)S(1)}, u32[]{:S(2)}, u32[]{:S(2)}) async-start(bf16[64,32,2,352]{3,1,2,0:T(8,128)(2,1)} %bitcast.50), calls=%async_computation.3 | async-start | bytes 6291456 | tf_op jit(solution)/shard_map/all_to_all | solution.py:56
  262.6 55.0 %all-to-all-start.7 = ((bf16[4,256,2048]{2,1,0:T(8,128)(2,1)}), bf16[4,256,2048]{2,1,0:T(8,128)(2,1)}, u32[]{:S(2)}, u32[]{:S(2)}) async-start(bf16[4,256,2048]{2,1,0:T(8,128)(2,1)} %stack.7), calls=%async_computation.8 | async-start | bytes 8388608 | tf_op jit(solution)/shard_map/all_to_all | solution.py:102
  323.5 133.2 %all-to-all-start.2 = ((bf16[4,512,2048]{2,1,0:T(8,128)(2,1)}), bf16[4,512,2048]{2,1,0:T(8,128)(2,1)}, u32[]{:S(2)}, u32[]{:S(2)}) async-start(bf16[4,512,2048]{2,1,0:T(8,128)(2,1)} %stack.6), calls=%async_computation.2 | async-start | bytes 16777216 | tf_op jit(solution)/shard_map/all_to_all | solution.py:102
  329.1 143.5 %reduce-scatter.6.cloned.1.call-start = ((), (), s32[]{:S(2)}) async-start(), calls=%async_computation.15 | async-start | bytes 5242880 | tf_op jit(solution)/shard_map/reduce_scatter | solution.py:104
  329.2 5.2 copy-start.3
  338.9 213.0 %reduce-scatter.4.cloned.1.call-start = ((), (), s32[]{:S(2)}) async-start(), calls=%async_computation.14 | async-start | bytes 10485760 | tf_op jit(solution)/shard_map/reduce_scatter | solution.py:104
  456.6 9.0 %copy-start.4 = (bf16[64,32,352]{2,1,0:T(8,128)(2,1)S(1)}, bf16[64,32,352]{2,1,0:T(8,128)(2,1)}, u32[]{:S(2)}) copy-start(bf16[64,32,352]{2,1,0:T(8,128)(2,1)} %copy-done.2) | copy-start | bytes 4325380
  472.6 9.5 %copy-start.13 = (bf16[256,2048]{1,0:T(8,128)(2,1)S(1)}, bf16[256,2048]{1,0:T(8,128)(2,1)}, u32[]{:S(2)}) copy-start(bf16[256,2048]{1,0:T(8,128)(2,1)} %all-gather.5.cloned.1.call-done) | copy-start | bytes 3145732
  475.0 35.9 %all-to-all-start.8 = ((bf16[64,4,2048]{2,1,0:T(4,128)(2,1)}), bf16[64,4,2048]{2,1,0:T(4,128)(2,1)S(1)}, u32[]{:S(2)}, u32[]{:S(2)}) async-start(bf16[64,4,2048]{2,1,0:T(4,128)(2,1)} %reshape.118), calls=%async_computation.10 | async-start | bytes 2097152 | tf_op jit(solution)/shard_map/all_to_all | solution.py:111
  551.8 61.8 %all-to-all-start.5 = ((bf16[64,8,2048]{2,1,0:T(8,128)(2,1)}), bf16[64,8,2048]{2,1,0:T(8,128)(2,1)S(1)}, u32[]{:S(2)}, u32[]{:S(2)}) async-start(bf16[64,8,2048]{2,1,0:T(8,128)(2,1)} %bitcast.53), calls=%async_computation.6 | async-start | bytes 4194304 | tf_op jit(solution)/shard_map/all_to_all | solution.py:111
  562.4 9.5 %copy-start.10 = (s32[64,6]{0,1:T(8,128)S(1)}, s32[64,6]{0,1:T(8,128)}, u32[]{:S(2)}) copy-start(s32[64,6]{0,1:T(8,128)} %param.16) | copy-start | bytes 4612
  562.4 58.8 %reduce-scatter.8.cloned.1.call-start = ((), (), s32[]{:S(2)}) async-start(), calls=%async_computation.16 | async-start | bytes 2621440 | tf_op jit(solution)/shard_map/reduce_scatter | solution.py:134
  621.1 3.8 copy-start.12
  624.2 0.7 copy-start.5
Sparse Core Ops, SparseCore 0:
  59.4 25.7 all-gather.4
  95.1 99.3 all-gather.6
  339.0 80.5 reduce-scatter.5
  472.7 79.0 reduce-scatter.3
  572.0 31.7 reduce-scatter.7
